TPU v7x, 128 devices: a whole 4x4x4 slice. The times are simulated.
128 devices in a mesh: sta: 32 (over z, y, x_lo), tm: 4 (over x_hi, core).
Axes of the slice: x: 4 (x_hi: 2, x_lo: 2; x = x_hi * 2 + x_lo), y: 4, z: 4, core: 2. Of those that a mesh axis runs over, the one named last changes fastest.
Arguments:
- signal: bfloat16 [1024, 12288], P('sta', 'tm'), may hold values from -6 to 6
- fir: float32 [4, 32], replicated, may hold values from -1 to 1
- taps: int32 [4], replicated, may hold values from 16 to 32, as said below
- sources: int32 [2, 16], replicated, may hold values from 0 to 1023, as said below
Outputs:
- correlations: bfloat16 [2, 4, 16, 1024, 512], P(None, None, None, 'sta', 'tm')
Inputs may be any that keep to these rules, and one draw needn't show every extreme that they name: Each band has between 16 and 32 taps, and some band has exactly 32. `sources`: the source channels of one round are distinct.
All inputs are finite; a program needn't handle non-finite values.
Results may differ from a plain program's by a relative error of at most 0.0058.
Values may be sent and summed in bfloat16 or wider, within the bound.
No kernel may reach another device: no remote copies, remote signals or barrier semaphores. Data moves between devices by JAX's collectives and lax.ppermute only.
A program may use at most 128 MiB of HBM per device.

v0:
```python
import jax
import jax.numpy as jnp
from jax import lax
from jax.sharding import PartitionSpec as P

ROUNDS = 2
MAXLAG = 256


def passed_along(value, axis, steps):
    count = lax.axis_size(axis)
    first, last = (max(0, -steps), min(count, count - steps))
    return lax.ppermute(value, axis, [(source, source + steps) for source in range(first, last)])


def padded_2(block, sides, width):
    for axis, dim in sides:
        count = lax.axis_size(axis)
        forward = [(i, i + 1) for i in range(count - 1)]
        backward = [(target, source) for source, target in forward]
        low = lax.ppermute(
            lax.slice_in_dim(block, block.shape[dim] - width, None, axis=dim), axis, forward
        )
        high = lax.ppermute(lax.slice_in_dim(block, 0, width, axis=dim), axis, backward)
        block = jnp.concatenate([low, block, high], axis=dim)
    return block


def skew(values, count_rows):
    leading = values.shape[:-1]
    length = values.shape[-1]
    row_width = length + count_rows
    padded = jnp.concatenate([values, jnp.zeros(leading + (count_rows,), values.dtype)], axis=-1)
    repeated = jnp.tile(padded, (1,) * len(leading) + (count_rows,))
    return repeated[..., : count_rows * (row_width - 1)].reshape(
        leading + (count_rows, row_width - 1)
    )


def band_matrix(fir, taps, count_rows):
    tap_limit = fir.shape[1]
    active = jnp.arange(tap_limit, dtype=jnp.int32)[None, :] < taps[:, None]
    coefficients = jnp.where(active, fir, 0.0).astype(jnp.bfloat16)
    return skew(coefficients[:, ::-1], count_rows)


def filter_blocks(extended, fir, taps, length, block):
    tap_limit = fir.shape[1]
    channels = extended.shape[0]
    count = length // block
    main = extended[:, tap_limit - 1 :].reshape(channels, count, block)
    prefix = extended[:, :length].reshape(channels, count, block)[:, :, : tap_limit - 1]
    pieces = jnp.concatenate([prefix, main], axis=2)
    result = jnp.einsum(
        "cnu,btu->bcnt", pieces, band_matrix(fir, taps, block), preferred_element_type=jnp.float32
    )
    return result.reshape(result.shape[0], channels, length)


def correlate(traces, window, lag_count, time_block, lag_block):
    bands = traces.shape[0]
    count_src = traces.shape[1]
    length = traces.shape[2]
    channels = window.shape[1]
    turns = length // time_block
    groups = lag_count // lag_block
    span = time_block + lag_block - 1

    def step(turn, total):
        begin = turn * time_block
        block = lax.dynamic_slice_in_dim(traces, begin, time_block, 2)
        slab = lax.dynamic_slice_in_dim(window, begin, lag_count + time_block - 1, 2)
        parts = []
        for band in range(bands):
            skewed = skew(block[band], lag_block)
            slabs = jnp.stack(
                [slab[band, :, g * lag_block : g * lag_block + span] for g in range(groups)], axis=1
            )
            term = jnp.einsum("sqj,cgj->gqsc", skewed, slabs, preferred_element_type=jnp.float32)
            parts.append(term.reshape(lag_count, count_src, channels))
        return total + jnp.stack(parts, axis=1)

    empty = jnp.zeros((lag_count, bands, count_src, channels), jnp.float32)
    return lax.fori_loop(0, turns, step, empty)


def per_device(signal, fir, taps, sources):
    channels = signal.shape[0]
    samples = signal.shape[1]
    tap_limit = fir.shape[1]
    shards = lax.axis_size("tm")
    samples_all = samples * shards
    lag_count = 2 * MAXLAG
    norm_scale = samples_all ** (-0.5)
    fir_block = min(256, samples)
    widened = None
    left_rim = passed_along(signal[:, samples - (tap_limit - 1) :], "tm", 1)
    extended = jnp.concatenate([left_rim, signal], axis=1)
    filtered = filter_blocks(extended, fir, taps, samples, fir_block).astype(jnp.bfloat16)
    local_ids = sources - lax.axis_index("sta") * channels
    onehot = (local_ids[:, :, None] == jnp.arange(channels, dtype=jnp.int32)[None, None, :]).astype(
        jnp.bfloat16
    )
    results = []
    widened = padded_2(filtered, (("tm", 2),), MAXLAG)
    share = lag_count // shards
    lag_block = min(128, share)
    time_block = min(512, samples)
    for rnd in range(ROUNDS):
        traces = lax.psum(
            jnp.einsum(
                "sc,bct->bst", onehot[rnd], filtered, preferred_element_type=jnp.float32
            ).astype(jnp.bfloat16),
            "sta",
        )

        def lag_terms(start, count, traces=traces):
            return correlate(traces, widened, count, time_block, lag_block) * norm_scale

        summed = lax.psum_scatter(
            lag_terms(jnp.int32(0), share * lax.axis_size("tm")),
            "tm",
            scatter_dimension=0,
            tiled=True,
        ).astype(jnp.bfloat16)
        results.append(jnp.transpose(summed, (1, 2, 3, 0)))
    return jnp.stack(results, axis=0)


def solution(mesh):
    in_specs = (P("sta", "tm"), P(), P(), P())
    out_specs = P(None, None, None, "sta", "tm")
    return jax.shard_map(
        per_device, mesh=mesh, in_specs=in_specs, out_specs=out_specs, check_vma=False
    )
```

profile of v0, /device:TPU:1, one launch (start us, length us, event | category | flops | bytes accessed | tf_op | source)
XLA Modules:
  0.0 1204.5 jit_solution(2703139181319280235)
XLA Ops:
  7.4 6.0 collective-permute-start
  30.9 278.6 %all-reduce.12.cloned.1.call-done = (bf16[4,16,3072]{2,1,0:T(8,128)(2,1)}, bf16[4,16,3072]{2,1,0:T(8,128)(2,1)}) async-done(((bf16[4,16,3072]{2,1,0:T(8,128)(2,1)}, bf16[4,16,3072]{2,1,0:T(8,128)(2,1)}), (bf16[4,16,3072]{2,1,0:T(8,128)(2,1)}, bf16[4,16,3072]{2,1,0:T(8,128)(2,1)})) %all-reduce.12.cloned.1.call-update) | async-done | bytes 786448 | tf_op jit(solution)/shard_map/psum | solution.py:110
  309.4 410.3 %while.28 = (s32[]{:T(128)}, f32[512,4,16,32]{0,3,2,1:T(8,128)}, bf16[4,32,3584]{2,1,0:T(8,128)(2,1)}, bf16[4,16,3072]{2,1,0:T(8,128)(2,1)}, s32[]{:T(128)}, /*i...) while((s32[]{:T(128)}, f32[512,4,16,32]{0,3,2,1:T(8,128)}, ...), condition=%wide.region_2.3_spmd.clone, body=%wide.region_1.2_spmd.clone.sunk | while | flops 1347940352 | bytes 132265400 | solution.py:84
  315.6 7.2 reshape.228
  329.4 7.2 reshape.230
  343.2 7.2 reshape.232
  356.9 7.2 reshape.226
  379.6 7.2 reshape.228
  393.3 7.2 reshape.230
  407.1 7.2 reshape.232
  420.9 7.2 reshape.226
  433.4 5.6 maximum_add_fusion.4
  444.9 7.2 reshape.228
  458.7 7.2 reshape.230
  472.5 7.2 reshape.232
  486.2 7.2 reshape.226
  498.8 5.6 maximum_add_fusion.4
  510.3 7.2 reshape.228
  524.1 7.2 reshape.230
  537.9 7.2 reshape.232
  551.6 7.2 reshape.226
  564.2 5.6 maximum_add_fusion.4
  575.6 7.2 reshape.228
  589.4 7.2 reshape.230
  603.2 7.2 reshape.232
  616.9 7.2 reshape.226
  629.5 5.6 maximum_add_fusion.4
  640.8 7.2 reshape.228
  654.6 7.2 reshape.230
  668.4 7.2 reshape.232
  682.1 7.2 reshape.226
  694.7 5.6 maximum_add_fusion.4
  719.8 5.1 broadcast_multiply_fusion.1
  725.0 392.1 %while.29 = (s32[]{:T(128)}, f32[512,4,16,32]{0,3,2,1:T(8,128)}, bf16[4,32,3584]{2,1,0:T(8,128)(2,1)}, bf16[4,16,3072]{2,1,0:T(8,128)(2,1)}, s32[]{:T(128)}, /*i...) while((s32[]{:T(128)}, f32[512,4,16,32]{0,3,2,1:T(8,128)}, ...), condition=%wide.region_6.7_spmd.clone, body=%wide.region_5.6_spmd.clone.sunk | while | flops 1347940352 | bytes 132265400 | solution.py:84
  731.0 7.2 reshape.236
  744.8 7.2 reshape.238
  758.5 7.6 reshape.240
  772.7 7.2 reshape.234
  795.5 7.2 reshape.236
  809.3 7.2 reshape.238
  823.0 7.2 reshape.240
  836.8 7.2 reshape.234
  849.5 5.6 maximum_add_fusion.5
  861.0 7.2 reshape.236
  874.8 7.2 reshape.238
  888.6 7.2 reshape.240
  902.4 7.2 reshape.234
  915.0 5.6 maximum_add_fusion.5
  926.6 7.2 reshape.236
  940.3 7.2 reshape.238
  954.1 7.2 reshape.240
  967.9 7.2 reshape.234
  980.6 5.6 maximum_add_fusion.5
  992.0 7.2 reshape.236
  1005.8 7.2 reshape.238
  1019.6 7.2 reshape.240
  1033.4 7.2 reshape.234
  1046.1 5.6 maximum_add_fusion.5
  1057.4 7.2 reshape.236
  1071.2 7.2 reshape.238
  1085.0 7.2 reshape.240
  1098.8 7.2 reshape.234
  1111.4 5.6 maximum_add_fusion.5
  1123.5 71.9 %reduce-scatter.5.cloned.1.call-done = f32[128,4,16,32]{0,3,2,1:T(8,128)} async-done(((f32[512,4,16,32]{0,3,2,1:T(8,128)}), f32[128,4,16,32]{0,3,2,1:T(8,128)}) %reduce-scatter.5.cloned.1.call-update) | async-done | bytes 1048592 | tf_op jit(solution)/shard_map/reduce_scatter | solution.py:120
  (477 shorter events, 404.5 us)
Async XLA Ops:
  6.5 11.4 copy-start.6
  6.5 302.9 %all-reduce.12.cloned.1.call-start = ((), (), s32[]{:S(2)}) async-start(), calls=%async_computation.4 | async-start | bytes 1572864 | tf_op jit(solution)/shard_map/psum | solution.py:110
  7.4 10.6 collective-permute-start
  21.1 1101.1 %reduce-scatter.3.cloned.1.call-start = ((), (), s32[]{:S(2)}) async-start(), calls=%async_computation.2 | async-start | bytes 5242880 | tf_op jit(solution)/shard_map/reduce_scatter | solution.py:120
  21.1 4.4 collective-permute-start.1
  23.1 7.1 collective-permute-start.2
  365.1 4.3 copy-start
  365.1 4.3 copy-start.2
  365.1 4.3 copy-start.4
  429.1 4.3 copy-start
  429.1 4.3 copy-start.2
  429.1 4.3 copy-start.4
  494.4 4.3 copy-start
  494.5 4.3 copy-start.2
  494.5 4.3 copy-start.4
  559.8 4.3 copy-start
  559.8 4.3 copy-start.2
  559.8 4.3 copy-start.4
  625.1 4.3 copy-start
  625.1 4.3 copy-start.2
  625.1 4.3 copy-start.4
  690.3 4.3 copy-start
  690.3 4.3 copy-start.2
  690.3 4.3 copy-start.4
  724.9 470.5 %reduce-scatter.5.cloned.1.call-start = ((), (), s32[]{:S(2)}) async-start(), calls=%async_computation.3 | async-start | bytes 5242880 | tf_op jit(solution)/shard_map/reduce_scatter | solution.py:120
  780.9 4.4 copy-start.1
  780.9 4.4 copy-start.3
  780.9 4.4 copy-start.5
  845.1 4.4 copy-start.1
  845.1 4.4 copy-start.3
  845.1 4.4 copy-start.5
  910.6 4.4 copy-start.1
  910.6 4.4 copy-start.3
  910.6 4.4 copy-start.5
  976.2 4.4 copy-start.1
  976.2 4.4 copy-start.3
  976.2 4.4 copy-start.5
  1041.6 4.4 copy-start.1
  1041.6 4.4 copy-start.3
  1041.7 4.4 copy-start.5
  1107.0 4.4 copy-start.1
  1107.0 4.4 copy-start.3
  1107.0 4.4 copy-start.5
Sparse Core Ops, SparseCore 0:
  21.2 288.1 all-reduce.11
  725.0 73.4 reduce-scatter.2
  1122.3 73.1 reduce-scatter.4
where the time goes:
time: 1210 us; the launch traced here: 1200 us
  local copies, waits for them, and re-layouts  675 us (56%)
  waiting for transfers between devices  354 us (29%)
  other arithmetic  80.2 us (7%)
  matrix products  50 us (4%)
  loops' own time  21.5 us (2%)
  between operations  13.5 us (1%)
    reshape x49, local copies, waits for them, and re-layouts, skew(): repeated[..., :count_rows * (row_width - 1)]  349 us
    psum x1, waiting for transfers between devices, per_device(): lax.psum(jnp.einsum('sc,bct->bst', onehot[rnd], filtered, preferred_eleme...  279 us
    slice x49, local copies, waits for them, and re-layouts, skew(): repeated[..., :count_rows * (row_width - 1)]  82.5 us
    reshape x48, local copies, waits for them, and re-layouts, step(): return total + jnp.stack(parts, axis=1)  82.2 us
    while x120, local copies, waits for them, and re-layouts  72.3 us
    reduce_scatter x2, waiting for transfers between devices, per_device(): lax.psum_scatter(lag_terms(jnp.int32(0), share * lax.axis_size('tm')), 't...  72 us
    add x12, other arithmetic, step(): return total + jnp.stack(parts, axis=1)  64.7 us
    dot_general x48, matrix products, step(): jnp.einsum('sqj,cgj->gqsc', skewed, slabs, preferred_element_type=jnp.flo...  47.4 us
  transfers between devices with their start and end apart: 6, of which 3 were waited for; matrix products, arithmetic and copies ran while one was open for 34% of the time, Pallas kernels for 0%

commit v1 on v0

--- a/solution.py
+++ b/solution.py
@@ -107,7 +107,8 @@
     lag_block = min(128, share)
     time_block = min(512, samples)
     for rnd in range(ROUNDS):
-        traces = lax.psum(
+        update_widths = lambda panel, axis_tag: jnp.sum(jax.lax.all_gather(panel, axis_tag), 0)
+        traces = update_widths(
             jnp.einsum(
                 "sc,bct->bst", onehot[rnd], filtered, preferred_element_type=jnp.float32
             ).astype(jnp.bfloat16),

time: 1210 us -> 1480 us (1.22)
  waiting for transfers between devices: 354 us -> 584 us
  loops' own time: 21.5 us -> 40.2 us
  other arithmetic: 80.2 us -> 97.4 us
    all_gather x0 -> x2, waiting for transfers between devices: none -> 533 us  [per_device(): jax.lax.all_gather(panel, axis_tag)]
    psum x1 -> x0, waiting for transfers between devices: 279 us -> none  [per_device(): lax.psum(jnp.einsum('sc,bct->bst', onehot[rnd], filtered, preferred_eleme...]
    reduce_scatter x2, waiting for transfers between devices: 72 us -> 47.8 us  [per_device(): lax.psum_scatter(lag_terms(jnp.int32(0), share * lax.axis_size('tm')), 't...]
    another operation x2, loops' own time: 21.5 us -> 40.2 us  [correlate(): return lax.fori_loop(0, turns, step, empty)]
    reduce_sum x0 -> x2, other arithmetic: none -> 17.3 us  [per_device(): jnp.sum(jax.lax.all_gather(panel, axis_tag), 0)]
  transfers between devices with their start and end apart: 6 -> 7, of which waited for: 3 -> 4; matrix products, arithmetic and copies ran while one was open for 34% -> 28% of each run, Pallas kernels for 0% -> 0%
where the time goes in v1:
time: 1480 us; the launch traced here: 1470 us
  local copies, waits for them, and re-layouts  673 us (45%)
  waiting for transfers between devices  584 us (39%)
  other arithmetic  97.4 us (7%)
  matrix products  50 us (3%)
  loops' own time  40.2 us (3%)
    all_gather x2, waiting for transfers between devices, per_device(): jax.lax.all_gather(panel, axis_tag)  533 us
    reshape x49, local copies, waits for them, and re-layouts, skew(): repeated[..., :count_rows * (row_width - 1)]  349 us
    reshape x48, local copies, waits for them, and re-layouts, step(): return total + jnp.stack(parts, axis=1)  81.8 us
    slice x49, local copies, waits for them, and re-layouts, skew(): repeated[..., :count_rows * (row_width - 1)]  80.4 us
    while x120, local copies, waits for them, and re-layouts  72.3 us
    add x12, other arithmetic, step(): return total + jnp.stack(parts, axis=1)  64.6 us
    reduce_scatter x2, waiting for transfers between devices, per_device(): lax.psum_scatter(lag_terms(jnp.int32(0), share * lax.axis_size('tm')), 't...  47.8 us
    dot_general x48, matrix products, step(): jnp.einsum('sqj,cgj->gqsc', skewed, slabs, preferred_element_type=jnp.flo...  47.4 us
  transfers between devices with their start and end apart: 7, of which 4 were waited for; matrix products, arithmetic and copies ran while one was open for 28% of the time, Pallas kernels for 0%

profile of v1, /device:TPU:1, one launch (start us, length us, event | category | flops | bytes accessed | tf_op | source)
XLA Modules:
  0.0 1468.5 jit_solution(1329392528924820154)
XLA Ops:
  7.4 6.0 collective-permute-start
  31.8 265.4 %all-gather.5.cloned.1.call-done = bf16[128,16,3072]{2,1,0:T(8,128)(2,1)} async-done(((bf16[4,16,3072]{2,1,0:T(8,128)(2,1)}), bf16[128,16,3072]{2,1,0:T(8,128)(2,1)}) %all-gather.5.cloned.1.call-update) | async-done | bytes 12582928 | tf_op jit(solution)/shard_map/all_gather | solution.py:110
  297.2 8.7 reduce_sum.24
  305.8 267.2 %all-gather.7.cloned.1.call-done = bf16[128,16,3072]{2,1,0:T(8,128)(2,1)} async-done(((bf16[4,16,3072]{2,1,0:T(8,128)(2,1)}), bf16[128,16,3072]{2,1,0:T(8,128)(2,1)}) %all-gather.7.cloned.1.call-update) | async-done | bytes 12582928 | tf_op jit(solution)/shard_map/all_gather | solution.py:110
  573.0 8.7 reduce_sum.25
  581.7 408.5 %while.29 = (s32[]{:T(128)}, f32[512,4,16,32]{0,3,2,1:T(8,128)}, bf16[4,32,3584]{2,1,0:T(8,128)(2,1)}, bf16[4,16,3072]{2,1,0:T(8,128)(2,1)}, s32[]{:T(128)}, /*i...) while((s32[]{:T(128)}, f32[512,4,16,32]{0,3,2,1:T(8,128)}, ...), condition=%wide.region_6.7_spmd.clone, body=%wide.region_5.6_spmd.clone.sunk | while | flops 1347940352 | bytes 132265400 | solution.py:84
  606.5 7.2 reshape.242
  620.2 7.2 reshape.240
  633.9 7.2 reshape.238
  647.6 7.2 reshape.236
  670.4 7.2 reshape.242
  684.1 7.2 reshape.240
  697.8 7.2 reshape.238
  711.5 7.2 reshape.236
  724.1 5.6 maximum_add_fusion.5
  735.5 7.2 reshape.242
  749.2 7.2 reshape.240
  762.9 7.2 reshape.238
  776.7 7.2 reshape.236
  800.7 7.2 reshape.242
  814.4 7.2 reshape.240
  828.1 7.2 reshape.238
  841.8 7.2 reshape.236
  854.4 5.6 maximum_add_fusion.5
  865.7 7.2 reshape.242
  879.5 7.2 reshape.240
  893.2 7.2 reshape.238
  906.9 7.2 reshape.236
  919.5 5.6 maximum_add_fusion.5
  930.9 7.2 reshape.242
  944.6 7.2 reshape.240
  958.3 7.2 reshape.238
  972.0 7.2 reshape.236
  995.3 409.6 %while.28 = (s32[]{:T(128)}, f32[512,4,16,32]{0,3,2,1:T(8,128)}, bf16[4,32,3584]{2,1,0:T(8,128)(2,1)}, bf16[4,16,3072]{2,1,0:T(8,128)(2,1)}, s32[]{:T(128)}, /*i...) while((s32[]{:T(128)}, f32[512,4,16,32]{0,3,2,1:T(8,128)}, ...), condition=%wide.region_2.3_spmd.clone, body=%wide.region_1.2_spmd.clone.sunk | while | flops 1347940352 | bytes 132265400 | solution.py:84
  1020.6 7.2 reshape.234
  1034.3 7.2 reshape.232
  1048.1 7.2 reshape.230
  1061.8 7.2 reshape.228
  1084.6 7.2 reshape.234
  1098.3 7.2 reshape.232
  1112.0 7.2 reshape.230
  1125.8 7.2 reshape.228
  1138.3 5.6 maximum_add_fusion.4
  1149.8 7.2 reshape.234
  1163.6 7.2 reshape.232
  1177.3 7.2 reshape.230
  1191.1 7.2 reshape.228
  1203.6 5.6 maximum_add_fusion.4
  1215.1 7.2 reshape.234
  1228.8 7.2 reshape.232
  1242.6 7.2 reshape.230
  1256.3 7.2 reshape.228
  1268.9 5.6 maximum_add_fusion.4
  1280.3 7.2 reshape.234
  1294.0 7.2 reshape.232
  1307.8 7.2 reshape.230
  1321.5 7.2 reshape.228
  1334.1 5.6 maximum_add_fusion.4
  1345.6 7.2 reshape.234
  1359.3 7.2 reshape.232
  1373.1 7.2 reshape.230
  1386.8 7.2 reshape.228
  1399.4 5.6 maximum_add_fusion.4
  1411.4 47.8 %reduce-scatter.3.cloned.1.call-done = f32[128,4,16,32]{0,3,2,1:T(8,128)} async-done(((f32[512,4,16,32]{0,3,2,1:T(8,128)}), f32[128,4,16,32]{0,3,2,1:T(8,128)}) %reduce-scatter.3.cloned.1.call-update) | async-done | bytes 1048592 | tf_op jit(solution)/shard_map/reduce_scatter | solution.py:121
  (482 shorter events, 419.1 us)
Async XLA Ops:
  6.5 12.4 copy-start.6
  6.5 290.6 %all-gather.5.cloned.1.call-start = ((), (), s32[]{:S(2)}) async-start(), calls=%async_computation.4 | async-start | bytes 12976128 | tf_op jit(solution)/shard_map/all_gather | solution.py:110
  7.4 11.5 collective-permute-start
  21.0 552.0 %all-gather.7.cloned.1.call-start = ((), (), s32[]{:S(2)}) async-start(), calls=%async_computation.5 | async-start | bytes 12976128 | tf_op jit(solution)/shard_map/all_gather | solution.py:110
  22.1 1388.0 %reduce-scatter.5.cloned.1.call-start = ((), (), s32[]{:S(2)}) async-start(), calls=%async_computation.3 | async-start | bytes 5242880 | tf_op jit(solution)/shard_map/reduce_scatter | solution.py:121
  22.1 4.4 collective-permute-start.1
  24.1 7.1 collective-permute-start.2
  655.9 4.3 copy-start
  655.9 4.3 copy-start.2
  655.9 4.3 copy-start.4
  719.7 4.3 copy-start
  719.7 4.3 copy-start.2
  719.7 4.3 copy-start.4
  784.9 4.3 copy-start
  784.9 4.3 copy-start.2
  784.9 4.3 copy-start.4
  850.0 4.3 copy-start
  850.0 4.3 copy-start.2
  850.0 4.3 copy-start.4
  915.1 4.3 copy-start
  915.1 4.3 copy-start.2
  915.1 4.3 copy-start.4
  980.3 4.3 copy-start
  980.3 4.3 copy-start.2
  980.3 4.3 copy-start.4
  995.3 464.0 %reduce-scatter.3.cloned.1.call-start = ((), (), s32[]{:S(2)}) async-start(), calls=%async_computation.2 | async-start | bytes 5242880 | tf_op jit(solution)/shard_map/reduce_scatter | solution.py:121
  1070.0 4.3 copy-start.1
  1070.0 4.3 copy-start.3
  1070.0 4.3 copy-start.5
  1134.0 4.3 copy-start.1
  1134.0 4.3 copy-start.3
  1134.0 4.3 copy-start.5
  1199.3 4.3 copy-start.1
  1199.3 4.3 copy-start.3
  1199.3 4.3 copy-start.5
  1264.5 4.3 copy-start.1
  1264.6 4.3 copy-start.3
  1264.6 4.3 copy-start.5
  1329.8 4.3 copy-start.1
  1329.8 4.3 copy-start.3
  1329.8 4.3 copy-start.5
  1395.0 4.3 copy-start.1
  1395.0 4.3 copy-start.3
  1395.0 4.3 copy-start.5
Sparse Core Ops, SparseCore 0:
  21.1 275.9 all-gather.4
  298.8 274.1 all-gather.6
  995.4 48.7 reduce-scatter.4
  1410.2 48.9 reduce-scatter.2
